TPU v7x, 128 devices: a whole 4x4x4 slice. The times are simulated.
128 devices in a mesh: guid: 2 (over x_hi), req: 4 (over x_lo, core), seq: 16 (over y, z).
Axes of the slice: x: 4 (x_hi: 2, x_lo: 2; x = x_hi * 2 + x_lo), y: 4, z: 4, core: 2. Of those that a mesh axis runs over, the one named last changes fastest.
Arguments:
- img_hidden: bfloat16 [2, 24, 1024, 1536], P('guid', 'req', 'seq'), may hold values from -6 to 6
- txt_hidden: bfloat16 [2, 24, 192, 1536], P('guid', 'req', 'seq'), may hold values from -6 to 6
- img_mod: float32 [2, 24, 5, 1536], P('guid', 'req')
- txt_mod: float32 [2, 24, 2, 1536], P('guid', 'req'), may hold values from -3 to 3
- w_img_qkv: bfloat16 [1536, 3072], P(('guid', 'req', 'seq')), may hold values from -0.15625 to 0.15625
- w_txt_qkv: bfloat16 [1536, 3072], P(('guid', 'req', 'seq')), may hold values from -0.15625 to 0.15625
- w_out: bfloat16 [1024, 1536], P(('guid', 'req', 'seq')), may hold values from -0.1875 to 0.1875
- w_head: bfloat16 [1536, 64], P(('guid', 'req', 'seq')), may hold values from -0.15625 to 0.15625
- text_lengths: int32 [2, 24], P('guid', 'req'), may hold values from 1 to 154, as said below
- latent: float32 [24, 1024, 64], P('req', 'seq', 'guid'), may hold values from -6 to 6
- step: int32 [1], replicated, may hold values from 0 to 27
Outputs:
- advanced: float32 [24, 1024, 64], P('req', 'seq', 'guid')
- guided: float32 [24, 1024, 64], P('req', 'seq', 'guid')
Inputs may be any that keep to these rules, and one draw needn't show every extreme that they name: `text_lengths`: in each half one prompt has 154 text tokens and another has 1.
All inputs are finite; a program needn't handle non-finite values.
Results may differ from a plain program's by a relative error of at most 0.012.
The roundings to bfloat16 on the way count: a program that leaves them out, or rounds other values in their place, can miss the bound.
Values may be sent and summed in bfloat16 or wider, within the bound.
No kernel may reach another device: no remote copies, remote signals or barrier semaphores. Data moves between devices by JAX's collectives and lax.ppermute only.
A program may use at most 192 MiB of HBM per device.

v0:
```python
import jax
import jax.numpy as jnp
from jax import lax
from jax.sharding import PartitionSpec as P

HD = 64
STEPS = 28
norm_epsilon = 1e-06
flow_shift = 3.0
guide_scale = 4.5


def partner(value, axis, bit):
    mask = 2**bit
    pairs = [(source, source ^ mask) for source in range(lax.axis_size(axis))]
    return lax.ppermute(value, axis, pairs)


def modulate(values_in, shift_vec, scale_vec):
    values_in = values_in.astype(jnp.float32)
    average = jnp.mean(values_in, axis=-1, keepdims=True)
    variance = jnp.mean((values_in - average) ** 2, axis=-1, keepdims=True)
    normed = (values_in - average) * lax.rsqrt(variance + norm_epsilon)
    return (normed * (1.0 + scale_vec[..., None, :]) + shift_vec[..., None, :]).astype(jnp.bfloat16)


def sigma_level(step_value):
    remaining = 1.0 - step_value / STEPS
    return flow_shift * remaining / (1.0 + (flow_shift - 1.0) * remaining)


def local(
    img_hidden,
    txt_hidden,
    img_mod,
    txt_mod,
    w_img_qkv,
    w_txt_qkv,
    w_out,
    w_head,
    text_lengths,
    latent,
    step,
):
    all_axes = ("guid", "req", "seq")
    prompts = img_hidden.shape[1]
    img_rows = img_hidden.shape[2]
    txt_rows = txt_hidden.shape[2]
    model_width = img_hidden.shape[3]
    nseq = lax.axis_size("seq")
    full_img = lax.all_gather(w_img_qkv, all_axes, axis=0, tiled=True)
    full_txt = lax.all_gather(w_txt_qkv, all_axes, axis=0, tiled=True)
    head_rows, head_cols = w_head.shape
    full_head = lax.all_gather(
        w_head.reshape(1, head_rows * head_cols), all_axes, axis=0, tiled=True
    ).reshape(-1, head_cols)
    full_out = lax.all_gather(w_out, all_axes, axis=0, tiled=True)
    image_in = modulate(img_hidden[0], img_mod[0, :, 0], img_mod[0, :, 1])
    text_in = modulate(txt_hidden[0], txt_mod[0, :, 0], txt_mod[0, :, 1])
    attn_width = full_img.shape[1] // 3
    head_count = attn_width // HD
    per_dev = head_count // nseq
    qkv_image = jnp.einsum(
        "prd,de->pre", image_in, full_img, preferred_element_type=jnp.float32
    ).astype(jnp.bfloat16)
    qkv_text = jnp.einsum(
        "prd,de->pre", text_in, full_txt, preferred_element_type=jnp.float32
    ).astype(jnp.bfloat16)
    img_split = qkv_image.reshape(prompts, img_rows, 3, nseq, per_dev * HD)
    img_heads = lax.all_to_all(img_split, "seq", 3, 1, tiled=True)
    txt_split = qkv_text[..., attn_width:].reshape(prompts, txt_rows, 2, nseq, per_dev * HD)
    txt_heads = lax.all_to_all(txt_split, "seq", 3, 1, tiled=True)
    all_img = img_heads.shape[1]
    all_txt = txt_heads.shape[1]
    query_heads = img_heads[:, :, 0, 0].reshape(prompts, all_img, per_dev, HD)
    key_heads = jnp.concatenate([img_heads[:, :, 1, 0], txt_heads[:, :, 0, 0]], axis=1).reshape(
        prompts, all_img + all_txt, per_dev, HD
    )
    value_heads = jnp.concatenate([img_heads[:, :, 2, 0], txt_heads[:, :, 1, 0]], axis=1).reshape(
        prompts, all_img + all_txt, per_dev, HD
    )
    lengths = text_lengths[0]
    scores = (
        jnp.einsum("pqhd,pkhd->phqk", query_heads, key_heads, preferred_element_type=jnp.float32)
        * 0.125
    )
    position = jnp.arange(all_img + all_txt, dtype=jnp.int32)
    allowed = (position < all_img)[None, :] | ((position - all_img)[None, :] < lengths[:, None])
    scores = jnp.where(allowed[:, None, None, :], scores, -1e30)
    highest = jnp.max(scores, axis=-1)
    weights = jnp.exp(scores - highest[..., None])
    totals = jnp.sum(weights, axis=-1)
    accumulated = jnp.einsum(
        "phqk,pkhd->pqhd",
        weights.astype(jnp.bfloat16),
        value_heads,
        preferred_element_type=jnp.float32,
    )
    mixture = accumulated / jnp.transpose(totals, (0, 2, 1))[..., None]
    head_out = mixture.astype(jnp.bfloat16).reshape(prompts, all_img, 1, per_dev * HD)
    token_out = lax.all_to_all(head_out, "seq", 1, 2, tiled=True)
    attended = token_out.reshape(prompts * img_rows, attn_width)
    projected = jnp.dot(attended, full_out, preferred_element_type=jnp.float32)
    residual = img_hidden[0].astype(jnp.float32) + img_mod[0, :, 2][:, None, :] * projected.reshape(
        prompts, img_rows, model_width
    )
    final_in = modulate(residual, img_mod[0, :, 3], img_mod[0, :, 4])
    guid_index = lax.axis_index("guid")
    half_width = latent.shape[2]
    own_start = guid_index * half_width
    other_start = (1 - guid_index) * half_width
    whole_velocity = jnp.einsum(
        "prd,dc->prc", final_in, full_head, preferred_element_type=jnp.float32
    )
    own_velocity = lax.dynamic_slice_in_dim(whole_velocity, own_start, half_width, 2)
    partner_part = lax.dynamic_slice_in_dim(whole_velocity, other_start, half_width, 2)
    other_velocity = partner(partner_part.astype(jnp.bfloat16), "guid", 0).astype(
        partner_part.dtype
    )
    cond_velocity = jnp.where(guid_index == 0, own_velocity, other_velocity)
    free_velocity = jnp.where(guid_index == 0, other_velocity, own_velocity)
    guided = free_velocity + guide_scale * (cond_velocity - free_velocity)
    step_value = step[0].astype(jnp.float32)
    advanced = latent + (sigma_level(step_value + 1.0) - sigma_level(step_value)) * guided
    return (advanced, guided)


def solution(mesh):
    placed = (
        P("guid", "req", "seq", None),
        P("guid", "req", "seq", None),
        P("guid", "req", None, None),
        P("guid", "req", None, None),
        P(("guid", "req", "seq"), None),
        P(("guid", "req", "seq"), None),
        P(("guid", "req", "seq"), None),
        P(("guid", "req", "seq"), None),
        P("guid", "req"),
        P("req", "seq", "guid"),
        P(),
    )
    return jax.shard_map(
        local,
        mesh=mesh,
        in_specs=placed,
        out_specs=(P("req", "seq", "guid"), P("req", "seq", "guid")),
        check_vma=False,
    )
```

profile of v0, /device:TPU:0, one launch (start us, length us, event | category | flops | bytes accessed | tf_op | source)
XLA Modules:
  0.0 415.2 jit_solution(12379703206547483496)
XLA Ops:
  14.4 72.3 %all-gather.11.cloned.1.call-done = bf16[128,12,3072]{2,1,0:T(8,128)(2,1)} async-done(((bf16[1,12,3072]{2,1,0:T(8,128)(2,1)}), bf16[128,12,3072]{2,1,0:T(8,128)(2,1)}) %all-gather.11.cloned.1.call-update) | async-done | bytes 9437200 | tf_op jit(solution)/shard_map/all_gather | solution.py:52
  86.7 13.7 %reshape.207 = bf16[1536,3072,1]{1,0,2:T(8,128)(2,1)} reshape(bf16[128,12,3072]{2,1,0:T(8,128)(2,1)} %all-gather.11.cloned.1.call-done) | data formatting | bytes 18874368
  100.4 5.4 %fusion.48 = bf16[6,12,3072]{2,1,0:T(8,128)(2,1)S(1)} fusion(bf16[1536,3072,1]{1,0,2:T(8,128)(2,1)} %reshape.207, bf16[1,6,12,1536]{3,2,1,0:T(8,128)(2,1)S(1)} %copy-done.1, f32[6,1536]{1,0:T(8,128)S(1)} %get-tuple-element.19, f32[6,1536]{1,0:T(8,128)S(1)} %get-tuple-element.20, f32[6,12]{1,0:T(8,128)S(1)} %add_rsqrt_fusion.1, ...), kind=kOutput, calls=%fused_computation.53 | convolution fusion | flops 680140800 | bytes 10175040 | tf_op jit(solution)/shard_map/prd,de->pre/dot_general | solution.py:66
  108.0 6.6 %all-to-all-start.1 = ((bf16[16,2,4608]{2,1,0:T(2,128)(2,1)}), bf16[16,2,4608]{2,1,0:T(2,128)(2,1)}, u32[]{:S(2)}, u32[]{:S(2)}) async-start(bf16[16,2,4608]{2,1,0:T(2,128)(2,1)} %reshape.213), calls=%async_computation.1 | async-start | bytes 589824 | tf_op jit(solution)/shard_map/all_to_all | solution.py:72
  114.6 47.7 %all-gather.9.cloned.1.call-done = bf16[128,12,3072]{2,1,0:T(8,128)(2,1)} async-done(((bf16[1,12,3072]{2,1,0:T(8,128)(2,1)}), bf16[128,12,3072]{2,1,0:T(8,128)(2,1)}) %all-gather.9.cloned.1.call-update) | async-done | bytes 9437200 | tf_op jit(solution)/shard_map/all_gather | solution.py:51
  162.3 13.7 %reshape.206 = bf16[1536,3072,1]{1,0,2:T(8,128)(2,1)} reshape(bf16[128,12,3072]{2,1,0:T(8,128)(2,1)} %all-gather.9.cloned.1.call-done) | data formatting | bytes 18874368
  176.0 8.2 %convolution_convert_fusion = bf16[6,64,3072]{2,1,0:T(8,128)(2,1)S(1)} fusion(bf16[1536,3072,1]{1,0,2:T(8,128)(2,1)} %reshape.206, bf16[1,6,64,1536]{3,2,1,0:T(8,128)(2,1)S(1)} %copy-done, f32[6,1536]{1,0:T(8,128)} %get-tuple-element.24, f32[6,1536]{1,0:T(8,128)} %get-tuple-element.23, f32[6,64]{1,0:T(8,128)S(1)} %add_rsqrt_fusion.2, ...), kind=kOutput, calls=%fused_computation.7 | convolution fusion | flops 3628597248 | bytes 13052928 | tf_op jit(solution)/shard_map/prd,de->pre/dot_general | solution.py:63
  184.2 4.8 %reshape.182 = bf16[6,64,3,16,64]{4,3,2,1,0:T(8,128)(2,1)} reshape(bf16[6,64,3072]{2,1,0:T(8,128)(2,1)S(1)} %convolution_convert_fusion) | data formatting | bytes 4718592 | tf_op jit(solution)/shard_map/reshape | solution.py:69
  189.0 5.7 %copy.84 = bf16[6,64,3,16,64]{4,1,2,0,3:T(8,128)(2,1)} copy(bf16[6,64,3,16,64]{4,3,2,1,0:T(8,128)(2,1)} %reshape.182) | data formatting | bytes 4718592 | tf_op jit(solution)/shard_map/reshape | solution.py:69
  194.7 7.8 %reshape.215 = bf16[16,2,36864]{2,1,0:T(2,128)(2,1)} reshape(bf16[16,6,3,64,64]{4,3,2,1,0:T(8,128)(2,1)} %bitcast.122) | data formatting | bytes 4718592
  202.6 6.7 %all-to-all-start = ((bf16[16,2,36864]{2,1,0:T(2,128)(2,1)}), bf16[16,2,36864]{2,1,0:T(2,128)(2,1)S(1)}, u32[]{:S(2)}, u32[]{:S(2)}) async-start(bf16[16,2,36864]{2,1,0:T(2,128)(2,1)} %reshape.215), calls=%async_computation | async-start | bytes 4718592 | tf_op jit(solution)/shard_map/all_to_all | solution.py:70
  220.0 23.2 %all-to-all-done = bf16[16,2,36864]{2,1,0:T(2,128)(2,1)S(1)} async-done(((bf16[16,2,36864]{2,1,0:T(2,128)(2,1)}), bf16[16,2,36864]{2,1,0:T(2,128)(2,1)S(1)}, u32[]{:S(2)}, u32[]{:S(2)}) %all-to-all-start) | async-done | bytes 2359328 | tf_op jit(solution)/shard_map/all_to_all | solution.py:70
  243.1 5.4 %reshape.216 = bf16[16,6,3,64,64]{4,3,2,1,0:T(8,128)(2,1)} reshape(bf16[16,2,36864]{2,1,0:T(2,128)(2,1)S(1)} %all-to-all-done) | data formatting | bytes 4718592
  248.5 6.1 %bitcast_bitcast_fusion = bf16[6,16,64,3,1,64]{5,2,3,0,1,4:T(8,128)(2,1)} fusion(bf16[16,6,3,64,64]{4,3,2,1,0:T(8,128)(2,1)} %reshape.216), kind=kLoop, calls=%fused_computation.92 | loop fusion | bytes 4718592 | tf_op jit(solution)/shard_map/all_to_all | solution.py:70
  254.6 7.3 %copy.44 = bf16[6,16,64,3,1,64]{2,1,5,0,3,4:T(8,128)(2,1)} copy(bf16[6,16,64,3,1,64]{5,2,3,0,1,4:T(8,128)(2,1)} %bitcast_bitcast_fusion) | data formatting | bytes 4718592 | tf_op jit(solution)/shard_map/all_to_all | solution.py:70
  261.9 6.3 %all_to_all.40 = bf16[6,1024,3,1,64]{1,4,0,3,2:T(8,128)(2,1)S(1)} reshape(bf16[6,16,64,3,1,64]{2,1,5,0,3,4:T(8,128)(2,1)} %copy.44) | data formatting | bytes 4718592 | tf_op jit(solution)/shard_map/all_to_all | solution.py:70
  269.1 11.0 %fusion = (f32[6,1024]{1,0:T(8,128)S(1)}, f32[6,1024,1216]{1,2,0:T(8,128)}) fusion(pred[6,1216]{1,0:T(8,128)(4,1)S(1)} %compare_or_fusion, bf16[6,192,64]{1,2,0:T(8,128)(2,1)S(1)} %bitcast.128, bf16[6,1024,64]{1,2,0:T(8,128)(2,1)S(1)} %get-tuple-element.5, bf16[6,1024,3,1,64]{1,4,0,3,2:T(8,128)(2,1)S(1)} %all_to_all.40), kind=kOutput, calls=%fused_computation.2 | convolution fusion | flops 980576256 | bytes 31688704 | tf_op jit(solution)/shard_map/pqhd,pkhd->phqk/dot_general | solution.py:84
  280.1 13.9 %fusion.1 = f32[6,1024]{1,0:T(8,128)S(1)} fusion(f32[6,1024,1216]{1,2,0:T(8,128)} %get-tuple-element.16, f32[6,1024]{1,0:T(8,128)S(1)} %get-tuple-element.15, pred[6,1216]{1,0:T(8,128)(4,1)S(1)} %compare_or_fusion), kind=kLoop, calls=%fused_computation.3 | loop fusion | flops 29878272 | bytes 29940864 | tf_op jit(solution)/shard_map/reduce_sum | solution.py:92
  294.1 13.4 %fusion.24 = bf16[6,1024,1,64]{1,3,0,2:T(8,128)(2,1)} fusion(f32[6,1024,1216]{1,2,0:T(8,128)} %get-tuple-element.16, f32[6,1024]{1,0:T(8,128)S(1)} %get-tuple-element.15, pred[6,1216]{1,0:T(8,128)(4,1)S(1)} %compare_or_fusion, bf16[6,192,64]{1,2,0:T(8,128)(2,1)S(1)} %bitcast.129, bf16[6,1024,64]{1,2,0:T(8,128)(2,1)S(1)} %get-tuple-element.4, ...), kind=kOutput, calls=%fused_computation.26 | convolution fusion | flops 988839936 | bytes 31661184 | tf_op jit(solution)/shard_map/phqk,pkhd->pqhd/dot_general | solution.py:93
  312.3 5.2 %all-to-all-start.2 = ((bf16[16,2,12288]{2,1,0:T(2,128)(2,1)}), bf16[16,2,12288]{2,1,0:T(2,128)(2,1)}, u32[]{:S(2)}, u32[]{:S(2)}) async-start(bf16[16,2,12288]{2,1,0:T(2,128)(2,1)} %reshape.217), calls=%async_computation.2 | async-start | bytes 1572864 | tf_op jit(solution)/shard_map/all_to_all | solution.py:101
  317.7 68.7 %all-gather.2 = bf16[128,1,768]{2,1,0:T(2,128)(2,1)S(1)} all-gather(bf16[1,1,768]{2,1,0:T(2,128)(2,1)S(1)} %reshape.202), channel_id=1, replica_groups=mesh['guid'=2,'req'=4,'seq'=16] {'guid','req','seq'}, dimensions={0}, use_global_device_ids=true | all-gather | bytes 198144 | tf_op jit(solution)/shard_map/all_gather | solution.py:54
  388.6 3.5 reshape.218
  397.0 3.4 fusion.68
  403.1 4.8 %collective-permute-done = bf16[6,64,32]{1,2,0:T(8,128)(2,1)S(1)} collective-permute-done((bf16[6,64,32]{1,2,0:T(8,128)(2,1)S(1)}, bf16[6,64,32]{1,2,0:T(8,128)(2,1)S(1)}, u32[]{:S(2)}, u32[]{:S(2)}) %collective-permute-start) | collective-permute-done | bytes 24608 | tf_op jit(solution)/shard_map/ppermute | solution.py:16
  (77 shorter events, 35.4 us)
Async XLA Ops:
  7.2 5.3 %copy-start = (bf16[1,6,64,1536]{3,2,1,0:T(8,128)(2,1)S(1)}, bf16[1,6,64,1536]{3,2,1,0:T(8,128)(2,1)}, u32[]{:S(2)}) copy-start(bf16[1,6,64,1536]{3,2,1,0:T(8,128)(2,1)} %param.11) | copy-start | bytes 3538948
  7.2 5.8 %copy-start.10 = (f32[1,6,2,1536]{3,2,1,0:T(2,128)S(1)}, f32[1,6,2,1536]{3,2,1,0:T(2,128)}, u32[]{:S(2)}) copy-start(f32[1,6,2,1536]{3,2,1,0:T(2,128)} %param.14) | copy-start | bytes 221188
  7.2 5.8 %copy-start.5 = (f32[1,6,5,1536]{3,0,2,1:T(1,128)S(1)}, f32[1,6,5,1536]{3,0,2,1:T(1,128)}, u32[]{:S(2)}) copy-start(f32[1,6,5,1536]{3,0,2,1:T(1,128)} %param.13) | copy-start | bytes 552964
  7.2 79.5 %all-gather.11.cloned.1.call-start = ((), (), s32[]{:S(2)}) async-start(), calls=%async_computation.5 | async-start | bytes 12681216 | tf_op jit(solution)/shard_map/all_gather | solution.py:52
  7.9 154.4 %all-gather.9.cloned.1.call-start = ((), (), s32[]{:S(2)}) async-start(), calls=%async_computation.4 | async-start | bytes 12681216 | tf_op jit(solution)/shard_map/all_gather | solution.py:51
  14.4 86.0 %copy-start.1 = (bf16[1,6,12,1536]{3,2,1,0:T(8,128)(2,1)S(1)}, bf16[1,6,12,1536]{3,2,1,0:T(8,128)(2,1)}, u32[]{:S(2)}) copy-start(bf16[1,6,12,1536]{3,2,1,0:T(8,128)(2,1)} %param.12) | copy-start | bytes 663556
  108.0 94.6 %all-to-all-start.1 = ((bf16[16,2,4608]{2,1,0:T(2,128)(2,1)}), bf16[16,2,4608]{2,1,0:T(2,128)(2,1)}, u32[]{:S(2)}, u32[]{:S(2)}) async-start(bf16[16,2,4608]{2,1,0:T(2,128)(2,1)} %reshape.213), calls=%async_computation.1 | async-start | bytes 589824 | tf_op jit(solution)/shard_map/all_to_all | solution.py:72
  202.6 7.4 %copy-start.12 = (s32[1,6]{1,0:T(1,128)S(1)}, s32[1,6]{1,0:T(1,128)}, u32[]{:S(2)}) copy-start(s32[1,6]{1,0:T(1,128)} %param.19) | copy-start | bytes 76
  202.6 40.5 %all-to-all-start = ((bf16[16,2,36864]{2,1,0:T(2,128)(2,1)}), bf16[16,2,36864]{2,1,0:T(2,128)(2,1)S(1)}, u32[]{:S(2)}, u32[]{:S(2)}) async-start(bf16[16,2,36864]{2,1,0:T(2,128)(2,1)} %reshape.215), calls=%async_computation | async-start | bytes 4718592 | tf_op jit(solution)/shard_map/all_to_all | solution.py:70
  209.3 187.7 %all-gather.7.cloned.1.call-start = ((), (), s32[]{:S(2)}) async-start(), calls=%async_computation.3 | async-start | bytes 3170304 | tf_op jit(solution)/shard_map/all_gather | solution.py:57
  268.2 0.9 copy-start.2
  280.1 14.0 %copy-start.4 = (bf16[6,192,1,1,64]{1,4,0,3,2:T(8,128)(2,1)S(1)}, bf16[6,192,1,1,64]{1,4,0,3,2:T(8,128)(2,1)}, u32[]{:S(2)}) copy-start(bf16[6,192,1,1,64]{1,4,0,3,2:T(8,128)(2,1)} %copy.63) | copy-start | bytes 442372
  310.1 7.5 %copy-start.8 = (f32[1,6,1,1536]{3,0,2,1:T(1,128)S(1)}, f32[1,6,1,1536]{3,0,2,1:T(1,128)}, u32[]{:S(2)}) copy-start(f32[1,6,1,1536]{3,0,2,1:T(1,128)} %get-tuple-element.10) | copy-start | bytes 110596
  310.1 7.5 %copy-start.11 = (bf16[12,64]{1,0:T(8,128)(2,1)S(1)}, bf16[12,64]{1,0:T(8,128)(2,1)}, u32[]{:S(2)}) copy-start(bf16[12,64]{1,0:T(8,128)(2,1)} %param.18) | copy-start | bytes 4612
  310.1 78.5 %copy-start.6 = (f32[1,6,1,1536]{3,0,2,1:T(1,128)S(1)}, f32[1,6,1,1536]{3,0,2,1:T(1,128)}, u32[]{:S(2)}) copy-start(f32[1,6,1,1536]{3,0,2,1:T(1,128)} %get-tuple-element.8) | copy-start | bytes 110596
  310.1 78.5 %copy-start.7 = (f32[1,6,1,1536]{3,0,2,1:T(1,128)S(1)}, f32[1,6,1,1536]{3,0,2,1:T(1,128)}, u32[]{:S(2)}) copy-start(f32[1,6,1,1536]{3,0,2,1:T(1,128)} %get-tuple-element.11) | copy-start | bytes 110596
  312.3 76.3 %all-to-all-start.2 = ((bf16[16,2,12288]{2,1,0:T(2,128)(2,1)}), bf16[16,2,12288]{2,1,0:T(2,128)(2,1)}, u32[]{:S(2)}, u32[]{:S(2)}) async-start(bf16[16,2,12288]{2,1,0:T(2,128)(2,1)} %reshape.217), calls=%async_computation.2 | async-start | bytes 1572864 | tf_op jit(solution)/shard_map/all_to_all | solution.py:101
  400.4 1.0 copy-start.3
  400.4 7.6 %copy-start.9 = (f32[6,64,32]{1,2,0:T(8,128)S(1)}, f32[6,64,32]{1,2,0:T(8,128)}, u32[]{:S(2)}) copy-start(f32[6,64,32]{1,2,0:T(8,128)} %param.20) | copy-start | bytes 147460
  402.3 5.7 %collective-permute-start = (bf16[6,64,32]{1,2,0:T(8,128)(2,1)S(1)}, bf16[6,64,32]{1,2,0:T(8,128)(2,1)S(1)}, u32[]{:S(2)}, u32[]{:S(2)}) collective-permute-start(bf16[6,64,32]{1,2,0:T(8,128)(2,1)S(1)} %dynamic-slice_convert_fusion), channel_id=1, source_target_pairs={{0,64},{64,0},{1,65},{65,1},{2,66},{66,2},{3,67},{67,3},{4,68},{68... | collective-permute-start | bytes 73736 | tf_op jit(solution)/shard_map/ppermute | solution.py:16
Sparse Core Ops, SparseCore 0:
  11.1 75.5 all-gather.10
  89.7 72.5 all-gather.8
  213.2 73.6 all-gather.6
where the time goes:
time: 417 us; the launch traced here: 415 us
  waiting for transfers between devices  150 us (36%)
  local copies, waits for them, and re-layouts  99.3 us (24%)
  blocking collectives  68.7 us (16%)
  matrix products  42.3 us (10%)
  other arithmetic  21.2 us (5%)
  starting transfers between devices  18.9 us (5%)
  between operations  14.9 us (4%)
    all_gather x1, waiting for transfers between devices, local(): full_txt = lax.all_gather(w_txt_qkv, all_axes, axis=0, tiled=True)  72.3 us
    all_gather x1, blocking collectives, local(): lax.all_gather(w_head.reshape(1, head_rows * head_cols), all_axes, axis=0...  68.7 us
    unnamed x38, local copies, waits for them, and re-layouts  54.8 us
    all_gather x1, waiting for transfers between devices, local(): full_img = lax.all_gather(w_img_qkv, all_axes, axis=0, tiled=True)  47.7 us
    all_to_all x1, waiting for transfers between devices, local(): img_heads = lax.all_to_all(img_split, 'seq', 3, 1, tiled=True)  23.2 us
    all_to_all x3, local copies, waits for them, and re-layouts, local(): img_heads = lax.all_to_all(img_split, 'seq', 3, 1, tiled=True)  19.7 us
    reduce_sum x1, other arithmetic, local(): totals = jnp.sum(weights, axis=-1)  13.9 us
    dot_general x1, matrix products, local(): jnp.einsum('phqk,pkhd->pqhd', weights.astype(jnp.bfloat16), value_heads,...  13.4 us
  transfers between devices with their start and end apart: 7, of which 4 were waited for; matrix products, arithmetic and copies ran while one was open for 36% of the time, Pallas kernels for 0%

commit v1 on v0

--- a/solution.py
+++ b/solution.py
@@ -49,7 +49,9 @@
     model_width = img_hidden.shape[3]
     nseq = lax.axis_size("seq")
     full_img = lax.all_gather(w_img_qkv, all_axes, axis=0, tiled=True)
-    full_txt = lax.all_gather(w_txt_qkv, all_axes, axis=0, tiled=True)
+    full_txt = jnp.concatenate(
+        lax.all_to_all(jnp.stack([w_txt_qkv] * lax.axis_size(all_axes)), all_axes, 0, 0), axis=0
+    )
     head_rows, head_cols = w_head.shape
     full_head = lax.all_gather(
         w_head.reshape(1, head_rows * head_cols), all_axes, axis=0, tiled=True

time: 417 us -> 480 us (1.15)
  waiting for transfers between devices: 150 us -> 187 us
  starting transfers between devices: 18.9 us -> 33.5 us
  local copies, waits for them, and re-layouts: 99.3 us -> 107 us
  blocking collectives: 68.7 us -> 74.6 us
    all_to_all x0 -> x1, waiting for transfers between devices: none -> 160 us  [local(): lax.all_to_all(jnp.stack([w_txt_qkv] * lax.axis_size(all_axes)), all_axes...]
    all_gather x1 -> x0, waiting for transfers between devices: 72.3 us -> none  [local(): full_txt = lax.all_gather(w_txt_qkv, all_axes, axis=0, tiled=True)]
    all_gather x1, waiting for transfers between devices: 47.7 us -> 0.02 us  [local(): full_img = lax.all_gather(w_img_qkv, all_axes, axis=0, tiled=True)]
    reshape x0 -> x1, local copies, waits for them, and re-layouts: none -> 14.4 us  [local(): jnp.concatenate(lax.all_to_all(jnp.stack([w_txt_qkv] * lax.axis_size(all_...]
    unnamed x38 -> x37, local copies, waits for them, and re-layouts: 54.8 us -> 41.1 us
    all_to_all x0 -> x1, starting transfers between devices: none -> 11.6 us  [local(): lax.all_to_all(jnp.stack([w_txt_qkv] * lax.axis_size(all_axes)), all_axes...]
    another operation x0 -> x1, local copies, waits for them, and re-layouts: none -> 7.09 us  [local(): jnp.stack([w_txt_qkv] * lax.axis_size(all_axes))]
    all_gather x1, blocking collectives: 68.7 us -> 74.6 us  [local(): lax.all_gather(w_head.reshape(1, head_rows * head_cols), all_axes, axis=0...]
  transfers between devices with their start and end apart: 7 -> 7, of which waited for: 4 -> 3; matrix products, arithmetic and copies ran while one was open for 36% -> 32% of each run, Pallas kernels for 0% -> 0%
where the time goes in v1:
time: 480 us; the launch traced here: 478 us
  waiting for transfers between devices  187 us (39%)
  local copies, waits for them, and re-layouts  107 us (22%)
  blocking collectives  74.6 us (16%)
  matrix products  42.6 us (9%)
  starting transfers between devices  33.5 us (7%)
  other arithmetic  18.1 us (4%)
  between operations  15.2 us (3%)
    all_to_all x1, waiting for transfers between devices, local(): lax.all_to_all(jnp.stack([w_txt_qkv] * lax.axis_size(all_axes)), all_axes...  160 us
    all_gather x1, blocking collectives, local(): lax.all_gather(w_head.reshape(1, head_rows * head_cols), all_axes, axis=0...  74.6 us
    unnamed x37, local copies, waits for them, and re-layouts  41.1 us
    all_to_all x1, waiting for transfers between devices, local(): img_heads = lax.all_to_all(img_split, 'seq', 3, 1, tiled=True)  20.5 us
    all_to_all x3, local copies, waits for them, and re-layouts, local(): img_heads = lax.all_to_all(img_split, 'seq', 3, 1, tiled=True)  19.7 us
    reshape x1, local copies, waits for them, and re-layouts, local(): jnp.concatenate(lax.all_to_all(jnp.stack([w_txt_qkv] * lax.axis_size(all_...  14.4 us
    reduce_sum x1, other arithmetic, local(): totals = jnp.sum(weights, axis=-1)  14 us
    dot_general x1, matrix products, local(): jnp.einsum('phqk,pkhd->pqhd', weights.astype(jnp.bfloat16), value_heads,...  13.4 us
  transfers between devices with their start and end apart: 7, of which 3 were waited for; matrix products, arithmetic and copies ran while one was open for 32% of the time, Pallas kernels for 0%

profile of v1, /device:TPU:0, one launch (start us, length us, event | category | flops | bytes accessed | tf_op | source)
XLA Modules:
  0.0 477.9 jit_solution(2232887923609762981)
XLA Ops:
  7.9 7.1 %stack.2 = bf16[128,12,3072]{2,1,0:T(8,128)(2,1)} broadcast(bf16[12,3072]{1,0:T(8,128)(2,1)} %param.16), dimensions={1,2} | broadcast | bytes 9510912 | tf_op jit(solution)/shard_map/stack | solution.py:53
  15.0 11.6 %all-to-all-start.1 = ((bf16[128,12,3072]{2,1,0:T(8,128)(2,1)}), bf16[128,12,3072]{2,1,0:T(8,128)(2,1)}, u32[]{:S(2)}, u32[]{:S(2)}) async-start(bf16[128,12,3072]{2,1,0:T(8,128)(2,1)} %stack.2), calls=%async_computation.1 | async-start | bytes 25165824 | tf_op jit(solution)/shard_map/all_to_all | solution.py:53
  29.1 160.3 %all-to-all-done.1 = bf16[128,12,3072]{2,1,0:T(8,128)(2,1)} async-done(((bf16[128,12,3072]{2,1,0:T(8,128)(2,1)}), bf16[128,12,3072]{2,1,0:T(8,128)(2,1)}, u32[]{:S(2)}, u32[]{:S(2)}) %all-to-all-start.1) | async-done | bytes 9437216 | tf_op jit(solution)/shard_map/all_to_all | solution.py:53
  189.4 14.4 %reshape.212 = bf16[1536,3072,1]{1,0,2:T(8,128)(2,1)} reshape(bf16[128,12,3072]{2,1,0:T(8,128)(2,1)} %all-to-all-done.1) | data formatting | bytes 18874368 | tf_op jit(solution)/shard_map/reshape | solution.py:52
  203.8 5.7 %fusion.49 = bf16[6,12,3072]{2,1,0:T(8,128)(2,1)S(1)} fusion(bf16[1536,3072,1]{1,0,2:T(8,128)(2,1)} %reshape.212, bf16[1,6,12,1536]{3,2,1,0:T(8,128)(2,1)S(1)} %copy-done.1, f32[6,1536]{1,0:T(8,128)S(1)} %get-tuple-element.19, f32[6,1536]{1,0:T(8,128)S(1)} %get-tuple-element.20, f32[6,12]{1,0:T(8,128)S(1)} %add_rsqrt_fusion.1, ...), kind=kOutput, calls=%fused_computation.55 | convolution fusion | flops 680140800 | bytes 10175040 | tf_op jit(solution)/shard_map/prd,de->pre/dot_general | solution.py:68
  211.7 9.9 %all-to-all-start.2 = ((bf16[16,2,4608]{2,1,0:T(2,128)(2,1)}), bf16[16,2,4608]{2,1,0:T(2,128)(2,1)}, u32[]{:S(2)}, u32[]{:S(2)}) async-start(bf16[16,2,4608]{2,1,0:T(2,128)(2,1)} %reshape.218), calls=%async_computation.2 | async-start | bytes 589824 | tf_op jit(solution)/shard_map/all_to_all | solution.py:74
  221.7 13.7 %reshape.211 = bf16[1536,3072,1]{1,0,2:T(8,128)(2,1)} reshape(bf16[128,12,3072]{2,1,0:T(8,128)(2,1)} %all-gather.7.cloned.1.call-done) | data formatting | bytes 18874368
  235.4 8.2 %convolution_convert_fusion = bf16[6,64,3072]{2,1,0:T(8,128)(2,1)S(1)} fusion(bf16[1536,3072,1]{1,0,2:T(8,128)(2,1)} %reshape.211, bf16[1,6,64,1536]{3,2,1,0:T(8,128)(2,1)S(1)} %copy-done, f32[6,1536]{1,0:T(8,128)} %get-tuple-element.24, f32[6,1536]{1,0:T(8,128)} %get-tuple-element.23, f32[6,64]{1,0:T(8,128)S(1)} %add_rsqrt_fusion.2, ...), kind=kOutput, calls=%fused_computation.7 | convolution fusion | flops 3628597248 | bytes 13052928 | tf_op jit(solution)/shard_map/prd,de->pre/dot_general | solution.py:65
  243.6 4.8 %reshape.188 = bf16[6,64,3,16,64]{4,3,2,1,0:T(8,128)(2,1)} reshape(bf16[6,64,3072]{2,1,0:T(8,128)(2,1)S(1)} %convolution_convert_fusion) | data formatting | bytes 4718592 | tf_op jit(solution)/shard_map/reshape | solution.py:71
  248.4 5.8 %copy.84 = bf16[6,64,3,16,64]{4,1,2,0,3:T(8,128)(2,1)} copy(bf16[6,64,3,16,64]{4,3,2,1,0:T(8,128)(2,1)} %reshape.188) | data formatting | bytes 4718592 | tf_op jit(solution)/shard_map/reshape | solution.py:71
  254.2 7.8 %reshape.220 = bf16[16,2,36864]{2,1,0:T(2,128)(2,1)} reshape(bf16[16,6,3,64,64]{4,3,2,1,0:T(8,128)(2,1)} %bitcast.115) | data formatting | bytes 4718592
  262.0 7.3 %all-to-all-start = ((bf16[16,2,36864]{2,1,0:T(2,128)(2,1)}), bf16[16,2,36864]{2,1,0:T(2,128)(2,1)S(1)}, u32[]{:S(2)}, u32[]{:S(2)}) async-start(bf16[16,2,36864]{2,1,0:T(2,128)(2,1)} %reshape.220), calls=%async_computation | async-start | bytes 4718592 | tf_op jit(solution)/shard_map/all_to_all | solution.py:72
  280.1 20.5 %all-to-all-done = bf16[16,2,36864]{2,1,0:T(2,128)(2,1)S(1)} async-done(((bf16[16,2,36864]{2,1,0:T(2,128)(2,1)}), bf16[16,2,36864]{2,1,0:T(2,128)(2,1)S(1)}, u32[]{:S(2)}, u32[]{:S(2)}) %all-to-all-start) | async-done | bytes 2359328 | tf_op jit(solution)/shard_map/all_to_all | solution.py:72
  300.6 5.3 %reshape.221 = bf16[16,6,3,64,64]{4,3,2,1,0:T(8,128)(2,1)} reshape(bf16[16,2,36864]{2,1,0:T(2,128)(2,1)S(1)} %all-to-all-done) | data formatting | bytes 4718592
  305.9 6.1 %bitcast_bitcast_fusion = bf16[6,16,64,3,1,64]{5,2,3,0,1,4:T(8,128)(2,1)} fusion(bf16[16,6,3,64,64]{4,3,2,1,0:T(8,128)(2,1)} %reshape.221), kind=kLoop, calls=%fused_computation.94 | loop fusion | bytes 4718592 | tf_op jit(solution)/shard_map/all_to_all | solution.py:72
  312.0 7.3 %copy.44 = bf16[6,16,64,3,1,64]{2,1,5,0,3,4:T(8,128)(2,1)} copy(bf16[6,16,64,3,1,64]{5,2,3,0,1,4:T(8,128)(2,1)} %bitcast_bitcast_fusion) | data formatting | bytes 4718592 | tf_op jit(solution)/shard_map/all_to_all | solution.py:72
  319.3 6.3 %all_to_all.43 = bf16[6,1024,3,1,64]{1,4,0,3,2:T(8,128)(2,1)S(1)} reshape(bf16[6,16,64,3,1,64]{2,1,5,0,3,4:T(8,128)(2,1)} %copy.44) | data formatting | bytes 4718592 | tf_op jit(solution)/shard_map/all_to_all | solution.py:72
  326.6 11.0 %fusion = (f32[6,1024]{1,0:T(8,128)S(1)}, f32[6,1024,1216]{1,2,0:T(8,128)}) fusion(pred[6,1216]{1,0:T(8,128)(4,1)S(1)} %compare_or_fusion, bf16[6,192,64]{1,2,0:T(8,128)(2,1)S(1)} %bitcast.121, bf16[6,1024,64]{1,2,0:T(8,128)(2,1)S(1)} %get-tuple-element.5, bf16[6,1024,3,1,64]{1,4,0,3,2:T(8,128)(2,1)S(1)} %all_to_all.43), kind=kOutput, calls=%fused_computation.2 | convolution fusion | flops 980576256 | bytes 31688704 | tf_op jit(solution)/shard_map/pqhd,pkhd->phqk/dot_general | solution.py:86
  337.6 14.0 %fusion.1 = f32[6,1024]{1,0:T(8,128)S(1)} fusion(f32[6,1024,1216]{1,2,0:T(8,128)} %get-tuple-element.16, f32[6,1024]{1,0:T(8,128)S(1)} %get-tuple-element.15, pred[6,1216]{1,0:T(8,128)(4,1)S(1)} %compare_or_fusion), kind=kLoop, calls=%fused_computation.3 | loop fusion | flops 29878272 | bytes 29940864 | tf_op jit(solution)/shard_map/reduce_sum | solution.py:94
  351.6 13.4 %fusion.24 = bf16[6,1024,1,64]{1,3,0,2:T(8,128)(2,1)} fusion(f32[6,1024,1216]{1,2,0:T(8,128)} %get-tuple-element.16, f32[6,1024]{1,0:T(8,128)S(1)} %get-tuple-element.15, pred[6,1216]{1,0:T(8,128)(4,1)S(1)} %compare_or_fusion, bf16[6,192,64]{1,2,0:T(8,128)(2,1)S(1)} %bitcast.122, bf16[6,1024,64]{1,2,0:T(8,128)(2,1)S(1)} %get-tuple-element.4, ...), kind=kOutput, calls=%fused_computation.26 | convolution fusion | flops 988839936 | bytes 31661184 | tf_op jit(solution)/shard_map/phqk,pkhd->pqhd/dot_general | solution.py:95
  369.9 4.3 all-to-all-start.3
  374.3 74.6 %all-gather.1 = bf16[128,1,768]{2,1,0:T(2,128)(2,1)S(1)} all-gather(bf16[1,1,768]{2,1,0:T(2,128)(2,1)S(1)} %reshape.207), channel_id=1, replica_groups=mesh['guid'=2,'req'=4,'seq'=16] {'guid','req','seq'}, dimensions={0}, use_global_device_ids=true | all-gather | bytes 198144 | tf_op jit(solution)/shard_map/all_gather | solution.py:56
  451.1 3.5 reshape.223
  465.6 4.8 %collective-permute-done = bf16[6,64,32]{1,2,0:T(8,128)(2,1)S(1)} collective-permute-done((bf16[6,64,32]{1,2,0:T(8,128)(2,1)S(1)}, bf16[6,64,32]{1,2,0:T(8,128)(2,1)S(1)}, u32[]{:S(2)}, u32[]{:S(2)}) %collective-permute-start) | collective-permute-done | bytes 24608 | tf_op jit(solution)/shard_map/ppermute | solution.py:16
  (77 shorter events, 34.9 us)
Async XLA Ops:
  7.2 214.5 %all-gather.7.cloned.1.call-start = ((), (), s32[]{:S(2)}) async-start(), calls=%async_computation.5 | async-start | bytes 12681216 | tf_op jit(solution)/shard_map/all_gather | solution.py:51
  15.0 11.7 %copy-start.1 = (bf16[1,6,12,1536]{3,2,1,0:T(8,128)(2,1)S(1)}, bf16[1,6,12,1536]{3,2,1,0:T(8,128)(2,1)}, u32[]{:S(2)}) copy-start(bf16[1,6,12,1536]{3,2,1,0:T(8,128)(2,1)} %param.12) | copy-start | bytes 663556
  15.0 12.0 %copy-start = (bf16[1,6,64,1536]{3,2,1,0:T(8,128)(2,1)S(1)}, bf16[1,6,64,1536]{3,2,1,0:T(8,128)(2,1)}, u32[]{:S(2)}) copy-start(bf16[1,6,64,1536]{3,2,1,0:T(8,128)(2,1)} %param.11) | copy-start | bytes 3538948
  15.0 174.4 %all-to-all-start.1 = ((bf16[128,12,3072]{2,1,0:T(8,128)(2,1)}), bf16[128,12,3072]{2,1,0:T(8,128)(2,1)}, u32[]{:S(2)}, u32[]{:S(2)}) async-start(bf16[128,12,3072]{2,1,0:T(8,128)(2,1)} %stack.2), calls=%async_computation.1 | async-start | bytes 25165824 | tf_op jit(solution)/shard_map/all_to_all | solution.py:53
  26.6 1.1 copy-start.10
  26.7 1.2 copy-start.5
  211.7 50.3 %all-to-all-start.2 = ((bf16[16,2,4608]{2,1,0:T(2,128)(2,1)}), bf16[16,2,4608]{2,1,0:T(2,128)(2,1)}, u32[]{:S(2)}, u32[]{:S(2)}) async-start(bf16[16,2,4608]{2,1,0:T(2,128)(2,1)} %reshape.218), calls=%async_computation.2 | async-start | bytes 589824 | tf_op jit(solution)/shard_map/all_to_all | solution.py:74
  262.0 8.1 %copy-start.12 = (s32[1,6]{1,0:T(1,128)S(1)}, s32[1,6]{1,0:T(1,128)}, u32[]{:S(2)}) copy-start(s32[1,6]{1,0:T(1,128)} %param.19) | copy-start | bytes 76
  262.0 38.5 %all-to-all-start = ((bf16[16,2,36864]{2,1,0:T(2,128)(2,1)}), bf16[16,2,36864]{2,1,0:T(2,128)(2,1)S(1)}, u32[]{:S(2)}, u32[]{:S(2)}) async-start(bf16[16,2,36864]{2,1,0:T(2,128)(2,1)} %reshape.220), calls=%async_computation | async-start | bytes 4718592 | tf_op jit(solution)/shard_map/all_to_all | solution.py:72
  269.3 190.1 %all-gather.5.cloned.1.call-start = ((), (), s32[]{:S(2)}) async-start(), calls=%async_computation.4 | async-start | bytes 3170304 | tf_op jit(solution)/shard_map/all_gather | solution.py:59
  325.6 0.9 copy-start.2
  337.6 14.0 %copy-start.4 = (bf16[6,192,1,1,64]{1,4,0,3,2:T(8,128)(2,1)S(1)}, bf16[6,192,1,1,64]{1,4,0,3,2:T(8,128)(2,1)}, u32[]{:S(2)}) copy-start(bf16[6,192,1,1,64]{1,4,0,3,2:T(8,128)(2,1)} %copy.63) | copy-start | bytes 442372
  367.6 6.5 %copy-start.8 = (f32[1,6,1,1536]{3,0,2,1:T(1,128)S(1)}, f32[1,6,1,1536]{3,0,2,1:T(1,128)}, u32[]{:S(2)}) copy-start(f32[1,6,1,1536]{3,0,2,1:T(1,128)} %get-tuple-element.10) | copy-start | bytes 110596
  367.6 6.6 %copy-start.11 = (bf16[12,64]{1,0:T(8,128)(2,1)S(1)}, bf16[12,64]{1,0:T(8,128)(2,1)}, u32[]{:S(2)}) copy-start(bf16[12,64]{1,0:T(8,128)(2,1)} %param.18) | copy-start | bytes 4612
  367.7 83.4 %copy-start.6 = (f32[1,6,1,1536]{3,0,2,1:T(1,128)S(1)}, f32[1,6,1,1536]{3,0,2,1:T(1,128)}, u32[]{:S(2)}) copy-start(f32[1,6,1,1536]{3,0,2,1:T(1,128)} %get-tuple-element.8) | copy-start | bytes 110596
  367.7 83.4 %copy-start.7 = (f32[1,6,1,1536]{3,0,2,1:T(1,128)S(1)}, f32[1,6,1,1536]{3,0,2,1:T(1,128)}, u32[]{:S(2)}) copy-start(f32[1,6,1,1536]{3,0,2,1:T(1,128)} %get-tuple-element.11) | copy-start | bytes 110596
  369.9 81.2 %all-to-all-start.3 = ((bf16[16,2,12288]{2,1,0:T(2,128)(2,1)}), bf16[16,2,12288]{2,1,0:T(2,128)(2,1)}, u32[]{:S(2)}, u32[]{:S(2)}) async-start(bf16[16,2,12288]{2,1,0:T(2,128)(2,1)} %reshape.222), calls=%async_computation.3 | async-start | bytes 1572864 | tf_op jit(solution)/shard_map/all_to_all | solution.py:103
  462.8 1.0 copy-start.3
  462.8 7.6 %copy-start.9 = (f32[6,64,32]{1,2,0:T(8,128)S(1)}, f32[6,64,32]{1,2,0:T(8,128)}, u32[]{:S(2)}) copy-start(f32[6,64,32]{1,2,0:T(8,128)} %param.20) | copy-start | bytes 147460
  464.7 5.7 %collective-permute-start = (bf16[6,64,32]{1,2,0:T(8,128)(2,1)S(1)}, bf16[6,64,32]{1,2,0:T(8,128)(2,1)S(1)}, u32[]{:S(2)}, u32[]{:S(2)}) collective-permute-start(bf16[6,64,32]{1,2,0:T(8,128)(2,1)S(1)} %dynamic-slice_convert_fusion), channel_id=1, source_target_pairs={{0,64},{64,0},{1,65},{65,1},{2,66},{66,2},{3,67},{67,3},{4,68},{68... | collective-permute-start | bytes 73736 | tf_op jit(solution)/shard_map/ppermute | solution.py:16
Sparse Core Ops, SparseCore 0:
  11.1 203.8 all-gather.6
  273.2 79.1 all-gather.4
